TPU v7x, 256 devices: a whole 4x4x8 slice. The times are simulated.
256 devices in a mesh: dp: 8 (over z), seq: 32 (over y, x, core).
Axes of the slice: x: 4, y: 4, z: 8, core: 2. Of those that a mesh axis runs over, the one named last changes fastest.
Arguments:
- inputs: bfloat16 [8, 4096, 2048], P('dp', 'seq'), may hold values from -6 to 6
- weight_codes: bfloat16 [2048, 1280], P('seq'), may hold values from -4 to 4
- scales: bfloat16 [2048, 10], P('seq'), may hold values from 0.010986328 to 0.043945312
- log_decay: float32 [8, 16, 4096], P('dp', None, 'seq'), may hold values from -0.85 to 0, as said below
- cotangent: bfloat16 [8, 4096, 1024], P('dp', 'seq'), may hold values from -6 to 6
Outputs:
- grad_inputs: float32 [8, 4096, 2048], P('dp', 'seq')
- grad_weight: float32 [2048, 1280], P('seq')
Inputs may be any that keep to these rules, and one draw needn't show every extreme that they name: log_decay is negative everywhere.
All inputs are finite; a program needn't handle non-finite values.
Results may differ from a plain program's by a relative error of at most 0.017.
Values may be sent and summed in bfloat16 or wider, within the bound.
No kernel may reach another device: no remote copies, remote signals or barrier semaphores. Data moves between devices by JAX's collectives and lax.ppermute only.
A program may use at most 128 MiB of HBM per device.

v0:
```python
import math
import jax
import jax.numpy as jnp
from jax import lax
from jax.sharding import PartitionSpec as P


def entering(part, axis, combine, identity, reverse):
    count = lax.axis_size(axis)
    place = lax.axis_index(axis)
    ahead = count - 1 - place if reverse else place
    gathered = jax.tree.map(lambda a: lax.all_gather(a, axis), part)
    state = jax.tree.map(lambda a, e: jnp.zeros_like(a) + jnp.asarray(e, a.dtype), part, identity)

    def one(hop, state):
        source = count - 1 - hop if reverse else hop
        return combine(
            state, jax.tree.map(lambda a: lax.dynamic_index_in_dim(a, source, 0, False), gathered)
        )

    return lax.fori_loop(0, ahead, one, state)


def dequantize(code_rows, scale_rows):
    row_count, col_count = code_rows.shape
    group_count = scale_rows.shape[1]
    spread = code_rows.astype(jnp.float32).reshape(row_count, group_count, col_count // group_count)
    spread = spread * scale_rows.astype(jnp.float32)[:, :, None]
    return spread.reshape(row_count, col_count).astype(jnp.bfloat16)


def block_prep(ld_block):
    cum_log = jnp.cumsum(ld_block, axis=1)
    input_scale = jnp.sqrt(-jnp.expm1(2.0 * ld_block))
    tail_weight = jnp.exp(cum_log[:, -1:] - cum_log) * input_scale
    return (cum_log, input_scale, tail_weight)


def weighted_pair(x_vals, grad_out, tail_weight, cum_log, inv_root):
    head_weight = jnp.exp(cum_log) * inv_root
    weighted_x = (x_vals.astype(jnp.float32) * tail_weight.T[:, :, None]).astype(jnp.bfloat16)
    weighted_g = (grad_out.astype(jnp.float32) * head_weight.T[:, :, None]).astype(jnp.bfloat16)
    return (weighted_x, weighted_g)


def summaries(x_vals, b_mat, c_mat, grad_out, ld_block):
    cum_log, input_scale, tail_weight = block_prep(ld_block)
    inv_root = 1.0 / math.sqrt(b_mat.shape[1])
    weighted_x, weighted_g = weighted_pair(x_vals, grad_out, tail_weight, cum_log, inv_root)
    fwd_state = jnp.einsum("sn,shp->hnp", b_mat, weighted_x, preferred_element_type=jnp.float32)
    back_state = jnp.einsum("tn,thp->hnp", c_mat, weighted_g, preferred_element_type=jnp.float32)
    return (jnp.exp(cum_log[:, -1]), fwd_state, back_state)


def block_grads(x_vals, b_mat, c_mat, grad_out, ld_block, state_in, back_in):
    block_len = ld_block.shape[1]
    cum_log, input_scale, tail_weight = block_prep(ld_block)
    inv_root = 1.0 / math.sqrt(b_mat.shape[1])
    weighted_x, weighted_g = weighted_pair(x_vals, grad_out, tail_weight, cum_log, inv_root)
    row_ids = lax.broadcasted_iota(jnp.int32, (block_len, block_len), 0)
    col_ids = lax.broadcasted_iota(jnp.int32, (block_len, block_len), 1)
    lower_mask = (row_ids >= col_ids)[None]
    log_gap = cum_log[:, :, None] - cum_log[:, None, :]
    decay_mat = jnp.where(lower_mask, jnp.exp(jnp.where(lower_mask, log_gap, 0.0)), 0.0)
    state_low = state_in.astype(jnp.bfloat16)
    back_low = back_in.astype(jnp.bfloat16)
    x_dot_g = jnp.einsum("thp,shp->hts", grad_out, x_vals, preferred_element_type=jnp.float32)
    c_dot_b = jnp.dot(c_mat, b_mat.T, preferred_element_type=jnp.float32)
    mix_weights = (
        jnp.sum(decay_mat * input_scale[:, None, :] * x_dot_g, axis=0) * inv_root
    ).astype(jnp.bfloat16)
    d_c = jnp.einsum("hnp,thp->tn", state_low, weighted_g, preferred_element_type=jnp.float32)
    d_c = d_c + jnp.dot(mix_weights, b_mat, preferred_element_type=jnp.float32)
    d_b = jnp.einsum("hnp,thp->tn", back_low, weighted_x, preferred_element_type=jnp.float32)
    d_b = d_b + jnp.dot(mix_weights.T, c_mat, preferred_element_type=jnp.float32)
    d_x = (
        jnp.einsum("tn,hnp->thp", b_mat, back_low, preferred_element_type=jnp.float32)
        * tail_weight.T[:, :, None]
    )
    inner_weights = (decay_mat * c_dot_b[None] * inv_root).astype(jnp.bfloat16)
    inner = jnp.einsum("hus,uhp->shp", inner_weights, grad_out, preferred_element_type=jnp.float32)
    d_x = d_x + input_scale.T[:, :, None] * inner
    return (d_x, d_b, d_c)


def state_chain(decays, adds, start, backward):

    def step(carry, item):
        return (item[0][:, None, None] * carry + item[1], carry)

    return lax.scan(step, start, (decays, adds), reverse=backward)


def join_summary(earlier, later):
    return (earlier[0] * later[0], later[0][:, None, None] * earlier[1] + later[1])


def local(inputs, weight_codes, scales, log_decay, cotangent):
    tok_count = inputs.shape[1]
    features = inputs[0]
    grad_out = cotangent[0]
    head_count = log_decay.shape[1]
    hp_width = grad_out.shape[1]
    head_dim = hp_width // head_count
    proj_width = weight_codes.shape[1]
    state_width = (proj_width - hp_width) // 2
    full_codes, full_scales = (
        lax.all_gather(weight_codes, "seq", axis=0, tiled=True),
        lax.all_gather(scales, "seq", axis=0, tiled=True),
    )
    weights = dequantize(full_codes, full_scales)
    projected = jnp.dot(features, weights, preferred_element_type=jnp.float32).astype(jnp.bfloat16)
    block_len = min(128, tok_count)
    block_count = tok_count // block_len
    x_blocks = projected[:, :hp_width].reshape(block_count, block_len, head_count, head_dim)
    b_blocks = projected[:, hp_width : hp_width + state_width].reshape(
        block_count, block_len, state_width
    )
    c_blocks = projected[:, hp_width + state_width :].reshape(block_count, block_len, state_width)
    g_blocks = grad_out.reshape(block_count, block_len, head_count, head_dim)
    ld_blocks = log_decay[0].reshape(head_count, block_count, block_len).transpose(1, 0, 2)
    decays, fwd_states, back_states = jax.vmap(summaries)(
        x_blocks, b_blocks, c_blocks, g_blocks, ld_blocks
    )
    zero_state = jnp.zeros((head_count, state_width, head_dim), jnp.float32)
    dev_decay = jnp.prod(decays, axis=0)
    dev_fwd, unused_a = state_chain(decays, fwd_states, zero_state, False)
    dev_back, unused_b = state_chain(decays, back_states, zero_state, True)
    neutral = (jnp.ones((head_count,), jnp.float32), zero_state)
    carried = entering((dev_decay, dev_fwd), "seq", join_summary, neutral, False)
    returned = entering((dev_decay, dev_back), "seq", join_summary, neutral, True)
    unused_c, state_starts = state_chain(decays, fwd_states, carried[1], False)
    unused_d, back_starts = state_chain(decays, back_states, returned[1], True)
    d_x, d_b, d_c = lax.map(
        lambda block_item: block_grads(*block_item),
        (x_blocks, b_blocks, c_blocks, g_blocks, ld_blocks, state_starts, back_starts),
    )
    d_proj = jnp.concatenate(
        [
            d_x.reshape(tok_count, hp_width),
            d_b.reshape(tok_count, state_width),
            d_c.reshape(tok_count, state_width),
        ],
        axis=1,
    ).astype(jnp.bfloat16)
    grad_in = lax.dot_general(
        d_proj, weights, (((1,), (1,)), ((), ())), preferred_element_type=jnp.float32
    )
    seq_count = lax.axis_size("seq")
    group_count = lax.axis_size("dp")
    norm_factor = 1.0 / math.sqrt(group_count * seq_count * tok_count)
    partial_grad = lax.psum_scatter(
        lax.dot_general(
            features, d_proj, (((0,), (0,)), ((), ())), preferred_element_type=jnp.float32
        ),
        "seq",
        scatter_dimension=0,
        tiled=True,
    )
    summed_grad = lax.psum(partial_grad, "dp")
    return (grad_in[None], summed_grad * norm_factor)


def solution(mesh):
    placed = (
        P("dp", "seq", None),
        P("seq", None),
        P("seq", None),
        P("dp", None, "seq"),
        P("dp", "seq", None),
    )
    return jax.shard_map(
        local,
        mesh=mesh,
        in_specs=placed,
        out_specs=(P("dp", "seq", None), P("seq", None)),
        check_vma=False,
    )
```

profile of v0, /device:TPU:2, one launch (start us, length us, event | category | flops | bytes accessed | tf_op | source)
XLA Modules:
  0.0 521.6 jit_solution(17085878530613788069)
XLA Ops:
  8.0 24.6 %all-gather.1 = bf16[32,64,10]{1,2,0:T(8,128)(2,1)S(1)} all-gather(bf16[1,64,10]{1,2,0:T(8,128)(2,1)} %bitcast.145), channel_id=1, replica_groups=mesh['dp'=8,'seq'=32] {'seq'}, dimensions={0}, use_global_device_ids=true | all-gather | bytes 42240 | tf_op jit(solution)/shard_map/all_gather | solution.py:109
  35.8 1.3 fusion.43
  37.1 28.6 %all-gather.6.cloned.1.call-done = bf16[2048,1280]{1,0:T(8,128)(2,1)} async-done(((bf16[64,1280]{1,0:T(8,128)(2,1)}), bf16[2048,1280]{1,0:T(8,128)(2,1)}) %all-gather.6.cloned.1.call-update) | async-done | bytes 5242896 | tf_op jit(solution)/shard_map/all_gather | solution.py:108
  65.7 7.9 %copy.59 = bf16[2048,1280]{0,1:T(8,128)(2,1)} copy(bf16[2048,1280]{1,0:T(8,128)(2,1)} %all-gather.6.cloned.1.call-done) | data formatting | bytes 10485760 | tf_op jit(solution)/shard_map/all_gather | solution.py:108
  73.6 3.9 fusion
  77.6 2.4 copy-done.2
  80.0 1.5 fusion.1
  85.5 21.4 %all-gather = f32[32,16,1]{1,2,0:T(1,128)} all-gather(f32[1,16,1]{1,2,0:T(1,128)S(1)} %exp.58), channel_id=2, replica_groups=mesh['dp'=8,'seq'=32] {'seq'}, dimensions={0}, use_global_device_ids=true | all-gather | bytes 2112 | tf_op jit(solution)/shard_map/all_gather | solution.py:12
  108.7 52.1 %all-gather.10.cloned.1.call-done = f32[32,16,128,64]{2,3,1,0:T(8,128)} async-done(((f32[1,16,128,64]{2,3,1,0:T(8,128)}), f32[32,16,128,64]{2,3,1,0:T(8,128)}) %all-gather.10.cloned.1.call-update) | async-done | bytes 16777232 | tf_op jit(solution)/shard_map/all_gather | solution.py:12
  160.9 4.7 while.17
  160.9 1.1 constant_dynamic-slice_fusion.5
  163.3 1.1 constant_dynamic-slice_fusion.5
  165.6 74.8 %all-gather.8.cloned.1.call-done = f32[32,16,128,64]{2,3,1,0:T(8,128)} async-done(((f32[1,16,128,64]{2,3,1,0:T(8,128)}), f32[32,16,128,64]{2,3,1,0:T(8,128)}) %all-gather.8.cloned.1.call-update) | async-done | bytes 16777232 | tf_op jit(solution)/shard_map/all_gather | solution.py:12
  240.5 68.7 %while.16 = (s32[]{:T(128)}, f32[16,128,64]{2,1,0:T(8,128)S(1)}, s32[]{:T(128)}, f32[32,16]{1,0:T(8,128)}, f32[32,16,128,64]{2,3,1,0:T(8,128)}, /*index=5*/s32[]{:T(128)}, s32[]{:T(128)}, s32[]{:T(128)}, s32[]{:T(128)}) while((s32[]{:T(128)}, f32[16,128,64]{2,1,0:T(8,128)S(1)}, s32[]{:T(128)}, f32[32,16]{1,0:T(8,128)}, ...), condition=%wide.region_2.3_spmd, body=%wide.region_1.2_spmd.sunk | while | flops 262150 | bytes 3670363 | solution.py:21
  245.3 1.1 constant_dynamic-slice_fusion.4
  247.7 1.1 constant_dynamic-slice_fusion.4
  250.1 1.1 constant_dynamic-slice_fusion.4
  252.4 1.1 constant_dynamic-slice_fusion.4
  254.8 1.1 constant_dynamic-slice_fusion.4
  257.2 1.1 constant_dynamic-slice_fusion.4
  273.7 1.1 constant_dynamic-slice_fusion.4
  276.1 1.1 constant_dynamic-slice_fusion.4
  278.4 1.1 constant_dynamic-slice_fusion.4
  309.6 1.2 convolution_bitcast_fusion.7
  310.8 1.5 convolution_bitcast_fusion.6
  313.5 5.3 %convolution_bitcast_fusion = f32[2048,1280]{0,1:T(8,128)} fusion(bf16[1,128,2048]{2,1,0:T(8,128)(2,1)S(1)} %copy-done, bf16[128,128]{0,1:T(8,128)(2,1)S(1)} %fusion.12, bf16[128,128]{0,1:T(8,128)(2,1)S(1)} %fusion.11, bf16[128,1024]{0,1:T(8,128)(2,1)S(1)} %bitcast.132), kind=kOutput, calls=%fused_computation.8 | convolution fusion | flops 672071680 | bytes 11337728 | tf_op jit(solution)/shard_map/dot_general | solution.py:153
  318.9 11.3 %copy.89 = f32[2048,1280]{1,0:T(8,128)} copy(f32[2048,1280]{0,1:T(8,128)} %convolution_bitcast_fusion) | data formatting | bytes 20971520
  330.2 106.7 %reduce-scatter.4.cloned.1.call-done = f32[64,1280]{1,0:T(8,128)} async-done(((f32[2048,1280]{1,0:T(8,128)}), f32[64,1280]{1,0:T(8,128)}) %reduce-scatter.4.cloned.1.call-update) | async-done | bytes 327696
  436.9 2.1 copy.90
  439.0 4.3 convolution_bitcast_fusion.1
  443.4 69.7 %all-reduce.2.cloned.1.call-done = f32[64,1280]{0,1:T(8,128)} async-done(((f32[64,1280]{0,1:T(8,128)}), f32[64,1280]{0,1:T(8,128)}) %all-reduce.2.cloned.1.call-update) | async-done | bytes 327696 | tf_op jit(solution)/shard_map/psum | solution.py:160
  513.0 1.1 broadcast_multiply_fusion
  (170 shorter events, 72.5 us)
Async XLA Ops:
  7.2 72.8 %copy-start = (bf16[1,128,2048]{2,1,0:T(8,128)(2,1)S(1)}, bf16[1,128,2048]{2,1,0:T(8,128)(2,1)}, u32[]{:S(2)}) copy-start(bf16[1,128,2048]{2,1,0:T(8,128)(2,1)} %param.9) | copy-start | bytes 1572868
  7.2 58.5 %all-gather.6.cloned.1.call-start = ((), (), s32[]{:S(2)}) async-start(), calls=%async_computation.1 | async-start | bytes 5406720 | tf_op jit(solution)/shard_map/all_gather | solution.py:108
  7.9 152.9 %all-gather.10.cloned.1.call-start = ((), (), s32[]{:S(2)}) async-start(), calls=%async_computation.3 | async-start | bytes 17301504 | tf_op jit(solution)/shard_map/all_gather | solution.py:12
  77.6 2.4 copy-start.2
  79.9 3.4 copy-start.5
  83.3 157.1 %all-gather.8.cloned.1.call-start = ((), (), s32[]{:S(2)}) async-start(), calls=%async_computation.2 | async-start | bytes 17301504 | tf_op jit(solution)/shard_map/all_gather | solution.py:12
  83.6 77.2 %copy-start.3 = (bf16[1,128,1024]{1,2,0:T(8,128)(2,1)}, bf16[1,128,1024]{1,2,0:T(8,128)(2,1)S(1)}, u32[]{:S(2)}) copy-start(bf16[1,128,1024]{1,2,0:T(8,128)(2,1)S(1)} %copy.63) | copy-start | bytes 786436
  85.4 351.5 %reduce-scatter.4.cloned.1.call-start = ((), (), s32[]{:S(2)}) async-start(), calls=%async_computation.5 | async-start | bytes 10813440
  106.9 53.9 %copy-start.7 = (pred[128,128]{0,1:T(8,128)(4,1)}, pred[128,128]{0,1:T(8,128)(4,1)S(1)}, u32[]{:S(2)}) copy-start(pred[128,128]{0,1:T(8,128)(4,1)S(1)} %iota_compare_fusion) | copy-start | bytes 49156
  165.6 74.9 %copy-start.1 = (f32[16,128,64]{2,1,0:T(8,128)}, f32[16,128,64]{2,1,0:T(8,128)S(1)}, u32[]{:S(2)}) copy-start(f32[16,128,64]{2,1,0:T(8,128)S(1)} %get-tuple-element.218) | copy-start | bytes 1572868
  309.2 3.7 copy-start.4
  309.2 3.7 copy-start.6
  309.2 3.7 copy-start.8
  309.3 3.7 copy-start.9
  330.2 182.8 %all-reduce.2.cloned.1.call-start = ((), (), s32[]{:S(2)}) async-start(), calls=%async_computation.4 | async-start | bytes 1310720 | tf_op jit(solution)/shard_map/psum | solution.py:160
Sparse Core Ops, SparseCore 0:
  10.6 55.0 all-gather.5
  83.4 77.2 all-gather.9
  163.3 77.0 all-gather.7
  330.3 106.5 reduce-scatter.3
  439.2 73.7 all-reduce.1
where the time goes:
time: 525 us; the launch traced here: 522 us
  waiting for transfers between devices  333 us (63%)
  local copies, waits for them, and re-layouts  91.1 us (17%)
  blocking collectives  46 us (9%)
  matrix products  18.9 us (4%)
  other arithmetic  17.6 us (3%)
  between operations  14 us (3%)
    all_gather x2, waiting for transfers between devices, entering(): gathered = jax.tree.map(lambda a: lax.all_gather(a, axis), part)  127 us
    unnamed x6, waiting for transfers between devices  107 us
    psum x1, waiting for transfers between devices, local(): summed_grad = lax.psum(partial_grad, 'dp')  69.7 us
    dynamic_slice x62, local copies, waits for them, and re-layouts, one(): lax.dynamic_index_in_dim(a, source, 0, False)  43.9 us
    all_gather x1, waiting for transfers between devices, local(): lax.all_gather(weight_codes, 'seq', axis=0, tiled=True)  28.6 us
    all_gather x1, blocking collectives, local(): lax.all_gather(scales, 'seq', axis=0, tiled=True)  24.6 us
    mul x31, local copies, waits for them, and re-layouts, join_summary(): later[0][:, None, None] * earlier[1] + later[1]  21.4 us
    all_gather x1, blocking collectives, entering(): gathered = jax.tree.map(lambda a: lax.all_gather(a, axis), part)  21.4 us
  transfers between devices with their start and end apart: 5, of which 5 were waited for; matrix products, arithmetic and copies ran while one was open for 3% of the time, Pallas kernels for 0%

commit v1 on v0

--- a/solution.py
+++ b/solution.py
@@ -1,8 +1,18 @@
+import functools
 import math
 import jax
 import jax.numpy as jnp
 from jax import lax
 from jax.sharding import PartitionSpec as P
+from jax.lax import all_to_all, axis_size
+
+
+def load_blocks_in(original, device_axis):
+    inter = jnp.concatenate([original for _ in range(axis_size(device_axis))], axis=0)
+    return all_to_all(inter, axis_name=device_axis, split_axis=0, concat_axis=0, tiled=True)
+
+
+_note_surface = functools.partial(load_blocks_in, device_axis="seq")
 
 
 def entering(part, axis, combine, identity, reverse):
@@ -105,7 +115,7 @@
     proj_width = weight_codes.shape[1]
     state_width = (proj_width - hp_width) // 2
     full_codes, full_scales = (
-        lax.all_gather(weight_codes, "seq", axis=0, tiled=True),
+        _note_surface(weight_codes),
         lax.all_gather(scales, "seq", axis=0, tiled=True),
     )
     weights = dequantize(full_codes, full_scales)

time: 525 us -> 604 us (1.15)
  waiting for transfers between devices: 333 us -> 276 us
  blocking collectives: 46 us -> 98.7 us
  local copies, waits for them, and re-layouts: 91.1 us -> 141 us
  other arithmetic: 17.6 us -> 34.5 us
  starting transfers between devices: 0.2 us -> 7.97 us
  matrix products: 18.9 us -> 25.4 us
    all_gather x2, waiting for transfers between devices: 127 us -> 61.4 us  [entering(): gathered = jax.tree.map(lambda a: lax.all_gather(a, axis), part)]
    all_gather x1, blocking collectives: 24.6 us -> 76.3 us  [local(): lax.all_gather(scales, 'seq', axis=0, tiled=True)]
    unnamed x6 -> x5, waiting for transfers between devices: 107 us -> 146 us
    all_gather x1 -> x0, waiting for transfers between devices: 28.6 us -> none  [local(): lax.all_gather(weight_codes, 'seq', axis=0, tiled=True)]
    convert_element_type x0 -> x2, local copies, waits for them, and re-layouts: none -> 23.8 us  [the longest x1 11.9 us: dequantize(): code_rows.astype(jnp.float32)]
    convert_element_type x1 -> x2, other arithmetic: 3.92 us -> 23.5 us  [dequantize(): return spread.reshape(row_count, col_count).astype(jnp.bfloat16)]
    unnamed x25 -> x57, local copies, waits for them, and re-layouts: 17 us -> 33.5 us
    mul x0 -> x2, local copies, waits for them, and re-layouts: none -> 16.5 us  [dequantize(): spread = spread * scale_rows.astype(jnp.float32)[:, :, None]]
  transfers between devices with their start and end apart: 5 -> 5, of which waited for: 5 -> 4; matrix products, arithmetic and copies ran while one was open for 3% -> 18% of each run, Pallas kernels for 0% -> 0%
where the time goes in v1:
time: 604 us; the launch traced here: 600 us
  waiting for transfers between devices  276 us (46%)
  local copies, waits for them, and re-layouts  141 us (23%)
  blocking collectives  98.7 us (16%)
  other arithmetic  34.5 us (6%)
  matrix products  25.4 us (4%)
  between operations  14.2 us (2%)
  starting transfers between devices  7.97 us (1%)
    unnamed x5, waiting for transfers between devices  146 us
    all_gather x1, blocking collectives, local(): lax.all_gather(scales, 'seq', axis=0, tiled=True)  76.3 us
    psum x1, waiting for transfers between devices, local(): summed_grad = lax.psum(partial_grad, 'dp')  68.7 us
    all_gather x2, waiting for transfers between devices, entering(): gathered = jax.tree.map(lambda a: lax.all_gather(a, axis), part)  61.4 us
    dynamic_slice x62, local copies, waits for them, and re-layouts, one(): lax.dynamic_index_in_dim(a, source, 0, False)  44.4 us
    unnamed x57, local copies, waits for them, and re-layouts  33.5 us
    convert_element_type x2, other arithmetic, dequantize(): return spread.reshape(row_count, col_count).astype(jnp.bfloat16)  23.5 us
    all_gather x1, blocking collectives, entering(): gathered = jax.tree.map(lambda a: lax.all_gather(a, axis), part)  22.3 us
  transfers between devices with their start and end apart: 5, of which 4 were waited for; matrix products, arithmetic and copies ran while one was open for 18% of the time, Pallas kernels for 0%

profile of v1, /device:TPU:2, one launch (start us, length us, event | category | flops | bytes accessed | tf_op | source)
XLA Modules:
  0.0 599.9 jit_solution(6400618546236057267)
XLA Ops:
  22.5 2.3 copy-done.4
  24.8 7.8 %all-to-all-start = ((bf16[32,64,1280]{2,1,0:T(8,128)(2,1)}), bf16[32,64,1280]{2,1,0:T(8,128)(2,1)}, u32[]{:S(2)}, u32[]{:S(2)}) async-start(bf16[32,64,1280]{2,1,0:T(8,128)(2,1)} %bitcast.137), calls=%async_computation | async-start | bytes 10485760 | tf_op jit(solution)/shard_map/all_to_all | solution.py:12
  33.4 76.3 %all-gather.1 = bf16[32,64,10]{1,2,0:T(8,128)(2,1)S(1)} all-gather(bf16[1,64,10]{1,2,0:T(8,128)(2,1)S(1)} %bitcast.152), channel_id=1, replica_groups=mesh['dp'=8,'seq'=32] {'seq'}, dimensions={0}, use_global_device_ids=true | all-gather | bytes 42240 | tf_op jit(solution)/shard_map/all_gather | solution.py:119
  112.1 11.9 %reshape.198 = f32[2048,10,128]{2,1,0:T(8,128)} reshape(bf16[32,64,1280]{2,1,0:T(8,128)(2,1)} %all-to-all-done) | data formatting | bytes 15728640 | tf_op jit(solution)/shard_map/convert_element_type | solution.py:37
  124.0 14.6 %multiply_convert_fusion = bf16[2048,10,128]{2,1,0:T(8,128)(2,1)} fusion(f32[2048,10,128]{2,1,0:T(8,128)} %reshape.198, f32[2048,10]{1,0:T(8,128)S(1)} %bitcast.135), kind=kLoop, calls=%fused_computation.6 | loop fusion | flops 5242880 | bytes 15810560 | tf_op jit(solution)/shard_map/convert_element_type | solution.py:39
  138.6 11.9 %copy.88 = bf16[2048,10,128]{0,2,1:T(8,128)(2,1)} copy(bf16[2048,10,128]{2,1,0:T(8,128)(2,1)} %multiply_convert_fusion) | data formatting | bytes 10485760 | tf_op jit(solution)/shard_map/convert_element_type | solution.py:39
  150.5 4.0 fusion.1
  157.5 22.3 %all-gather = f32[32,16,1]{1,2,0:T(1,128)} all-gather(f32[1,16,1]{1,2,0:T(1,128)S(1)} %exp.58), channel_id=2, replica_groups=mesh['dp'=8,'seq'=32] {'seq'}, dimensions={0}, use_global_device_ids=true | all-gather | bytes 2112 | tf_op jit(solution)/shard_map/all_gather | solution.py:22
  181.7 54.0 %all-gather.5.cloned.1.call-done = f32[32,16,128,64]{2,3,1,0:T(8,128)} async-done(((f32[1,16,128,64]{2,3,1,0:T(8,128)}), f32[32,16,128,64]{2,3,1,0:T(8,128)}) %all-gather.5.cloned.1.call-update) | async-done | bytes 16777232 | tf_op jit(solution)/shard_map/all_gather | solution.py:22
  235.8 69.3 %while.16 = (s32[]{:T(128)}, f32[16,128,64]{2,1,0:T(8,128)S(1)}, s32[]{:T(128)}, f32[32,16]{1,0:T(8,128)}, f32[32,16,128,64]{2,3,1,0:T(8,128)}, /*index=5*/s32[]{:T(128)}, s32[]{:T(128)}, s32[]{:T(128)}, s32[]{:T(128)}) while((s32[]{:T(128)}, f32[16,128,64]{2,1,0:T(8,128)S(1)}, s32[]{:T(128)}, f32[32,16]{1,0:T(8,128)}, ...), condition=%wide.region_2.3_spmd, body=%wide.region_1.2_spmd.sunk | while | flops 262150 | bytes 3670355 | solution.py:31
  250.1 1.1 constant_dynamic-slice_fusion.4
  276.2 1.2 constant_dynamic-slice_fusion.4
  283.5 1.1 constant_dynamic-slice_fusion.4
  285.9 1.1 constant_dynamic-slice_fusion.4
  302.6 1.2 constant_dynamic-slice_fusion.4
  306.1 1.9 convolution_bitcast_fusion.7
  307.9 7.4 %all-gather.7.cloned.1.call-done = f32[32,16,128,64]{2,3,1,0:T(8,128)} async-done(((f32[1,16,128,64]{2,3,1,0:T(8,128)}), f32[32,16,128,64]{2,3,1,0:T(8,128)}) %all-gather.7.cloned.1.call-update) | async-done | bytes 16777232 | tf_op jit(solution)/shard_map/all_gather | solution.py:22
  315.5 4.9 while.17
  321.4 1.2 convolution_bitcast_fusion.6
  322.8 1.2 fusion.32
  323.9 1.6 fusion.10
  325.5 5.3 convolution_bitcast_fusion
  330.8 11.3 %copy.120 = f32[2048,1280]{1,0:T(8,128)} copy(f32[2048,1280]{0,1:T(8,128)} %convolution_bitcast_fusion) | data formatting | bytes 20971520
  342.2 1.1 copy-done.3
  343.7 5.3 mul.263.clone
  349.0 11.2 %copy.106 = f32[2048,1280]{1,0:T(8,128)} copy(f32[2048,1280]{0,1:T(8,128)} %bitcast.134) | data formatting | bytes 20971520 | tf_op jit(solution)/shard_map/mul | solution.py:38
  360.2 8.9 %fusion = bf16[2048,1280]{1,0:T(8,128)(2,1)} fusion(f32[2048,1280]{1,0:T(8,128)} %copy.106, bf16[32,64,1280]{2,1,0:T(8,128)(2,1)} %all-to-all-done), kind=kLoop, calls=%fused_computation.8 | loop fusion | flops 7864320 | bytes 20971520 | tf_op jit(solution)/shard_map/convert_element_type | solution.py:39
  369.1 146.1 %reduce-scatter.4.cloned.1.call-done = f32[64,1280]{1,0:T(8,128)} async-done(((f32[2048,1280]{1,0:T(8,128)}), f32[64,1280]{1,0:T(8,128)}) %reduce-scatter.4.cloned.1.call-update) | async-done | bytes 327696
  515.2 2.1 copy.121
  517.3 5.3 convolution_bitcast_fusion.1
  522.6 68.7 %all-reduce.2.cloned.1.call-done = f32[64,1280]{0,1:T(8,128)} async-done(((f32[64,1280]{0,1:T(8,128)}), f32[64,1280]{0,1:T(8,128)}) %all-reduce.2.cloned.1.call-update) | async-done | bytes 327696 | tf_op jit(solution)/shard_map/psum | solution.py:170
  591.3 1.1 broadcast_multiply_fusion
  (206 shorter events, 93.3 us)
Async XLA Ops:
  7.2 143.3 %copy-start = (bf16[1,128,2048]{2,1,0:T(8,128)(2,1)S(1)}, bf16[1,128,2048]{2,1,0:T(8,128)(2,1)}, u32[]{:S(2)}) copy-start(bf16[1,128,2048]{2,1,0:T(8,128)(2,1)} %param.9) | copy-start | bytes 1572868
  7.2 15.0 %copy-start.1 = (bf16[64,1280]{1,0:T(8,128)(2,1)S(1)}, bf16[64,1280]{1,0:T(8,128)(2,1)}, u32[]{:S(2)}) copy-start(bf16[64,1280]{1,0:T(8,128)(2,1)} %param.10) | copy-start | bytes 491524
  22.5 2.3 copy-start.4
  24.8 7.9 %copy-start.7 = (f32[1,16,128]{2,1,0:T(8,128)S(1)}, f32[1,16,128]{2,1,0:T(8,128)}, u32[]{:S(2)}) copy-start(f32[1,16,128]{2,1,0:T(8,128)} %param.12) | copy-start | bytes 24580
  24.8 8.3 %copy-start.6 = (bf16[1,128,1024]{2,1,0:T(8,128)(2,1)S(1)}, bf16[1,128,1024]{2,1,0:T(8,128)(2,1)}, u32[]{:S(2)}) copy-start(bf16[1,128,1024]{2,1,0:T(8,128)(2,1)} %param.13) | copy-start | bytes 786436
  24.8 8.5 %copy-start.9 = (bf16[64,10]{0,1:T(8,128)(2,1)S(1)}, bf16[64,10]{0,1:T(8,128)(2,1)}, u32[]{:S(2)}) copy-start(bf16[64,10]{0,1:T(8,128)(2,1)} %param.11) | copy-start | bytes 3844
  24.8 87.2 %all-to-all-start = ((bf16[32,64,1280]{2,1,0:T(8,128)(2,1)}), bf16[32,64,1280]{2,1,0:T(8,128)(2,1)}, u32[]{:S(2)}, u32[]{:S(2)}) async-start(bf16[32,64,1280]{2,1,0:T(8,128)(2,1)} %bitcast.137), calls=%async_computation | async-start | bytes 10485760 | tf_op jit(solution)/shard_map/all_to_all | solution.py:12
  32.6 203.1 %all-gather.5.cloned.1.call-start = ((), (), s32[]{:S(2)}) async-start(), calls=%async_computation.2 | async-start | bytes 17301504 | tf_op jit(solution)/shard_map/all_gather | solution.py:22
  33.3 146.6 %copy-start.5 = (bf16[1,128,1024]{1,2,0:T(8,128)(2,1)}, bf16[1,128,1024]{1,2,0:T(8,128)(2,1)S(1)}, u32[]{:S(2)}) copy-start(bf16[1,128,1024]{1,2,0:T(8,128)(2,1)S(1)} %copy.91) | copy-start | bytes 786436
  110.1 13.9 %copy-start.2 = (f32[32,64,10]{2,1,0:T(8,128)}, f32[32,64,10]{2,1,0:T(8,128)S(1)}, u32[]{:S(2)}) copy-start(f32[32,64,10]{2,1,0:T(8,128)S(1)} %copy.115) | copy-start | bytes 245764
  155.6 159.8 %all-gather.7.cloned.1.call-start = ((), (), s32[]{:S(2)}) async-start(), calls=%async_computation.3 | async-start | bytes 17301504 | tf_op jit(solution)/shard_map/all_gather | solution.py:22
  157.5 357.8 %reduce-scatter.4.cloned.1.call-start = ((), (), s32[]{:S(2)}) async-start(), calls=%async_computation.5 | async-start | bytes 10813440
  179.9 55.9 %copy-start.8 = (pred[128,128]{0,1:T(8,128)(4,1)}, pred[128,128]{0,1:T(8,128)(4,1)S(1)}, u32[]{:S(2)}) copy-start(pred[128,128]{0,1:T(8,128)(4,1)S(1)} %iota_compare_fusion) | copy-start | bytes 49156
  342.1 1.2 copy-start.3
  342.2 249.1 %all-reduce.2.cloned.1.call-start = ((), (), s32[]{:S(2)}) async-start(), calls=%async_computation.4 | async-start | bytes 1310720 | tf_op jit(solution)/shard_map/psum | solution.py:170
Sparse Core Ops, SparseCore 0:
  155.7 79.9 all-gather.4
  238.3 77.0 all-gather.6
  342.3 172.9 reduce-scatter.3
  517.6 73.7 all-reduce.1
